TPU v7x, 128 devices: a whole 4x4x4 slice. The times are simulated.
128 devices in a mesh: ctx: 32 (over z, y_hi, x), ch: 4 (over y_lo, core).
Axes of the slice: x: 4, y: 4 (y_hi: 2, y_lo: 2; y = y_hi * 2 + y_lo), z: 4, core: 2. Of those that a mesh axis runs over, the one named last changes fastest.
Arguments:
- q_conv: bfloat16 [7168, 4096], P('ctx', 'ch'), may hold values from -6 to 6
- k_conv: bfloat16 [7168, 4096], P('ctx', 'ch'), may hold values from -6 to 6
- v_conv: bfloat16 [7168, 4096], P('ctx', 'ch'), may hold values from -6 to 6
- conv_filter: bfloat16 [7168, 256], P('ctx', 'ch'), may hold values from -1 to 1
- q_attn: bfloat16 [7168, 4096], P('ctx', 'ch'), may hold values from -5 to 5
- k_attn: bfloat16 [7168, 4096], P('ctx', 'ch'), may hold values from -5 to 5
- v_attn: bfloat16 [7168, 4096], P('ctx', 'ch'), may hold values from -6 to 6
- w_conv_out: bfloat16 [4096, 4096], P('ch'), may hold values from -0.09375 to 0.09375
- w_attn_out: bfloat16 [4096, 4096], P('ch'), may hold values from -0.375 to 0.375
Outputs:
- layer_out: bfloat16 [7168, 4096], P(('ctx', 'ch'))
All inputs are finite; a program needn't handle non-finite values.
Results may differ from a plain program's by a relative error of at most 0.018.
Values may be sent and summed in bfloat16 or wider, within the bound.
No kernel may reach another device: no remote copies, remote signals or barrier semaphores. Data moves between devices by JAX's collectives and lax.ppermute only.
A program may use at most 192 MiB of HBM per device.

v0:
```python
from functools import partial
import math
import jax
import jax.numpy as jnp
from jax import lax
from jax.sharding import PartitionSpec as P

HD = 128
two_pi = 2.0 * math.pi
neg_large = -1e30
highest = lax.Precision.HIGHEST


def angle_table(left_idx, right_idx, period):
    product = left_idx[:, None] * right_idx[None, :] % period
    return product.astype(jnp.float32) * (two_pi / period)


def section_coarse(values, cos_table, sin_table, twiddle):
    real_part = jnp.einsum("kn,nsc->ksc", cos_table, values, precision=highest)
    imag_part = -jnp.einsum("kn,nsc->ksc", sin_table, values, precision=highest)
    cos_twist = jnp.cos(twiddle)[:, :, None]
    sin_twist = jnp.sin(twiddle)[:, :, None]
    return (
        real_part * cos_twist + imag_part * sin_twist,
        imag_part * cos_twist - real_part * sin_twist,
    )


def section_fine(real_part, imag_part, cos_table, sin_table, direction):
    cos_real = jnp.einsum("kn,anc->akc", cos_table, real_part, precision=highest)
    cos_imag = jnp.einsum("kn,anc->akc", cos_table, imag_part, precision=highest)
    sin_real = jnp.einsum("kn,anc->akc", sin_table, real_part, precision=highest)
    sin_imag = jnp.einsum("kn,anc->akc", sin_table, imag_part, precision=highest)
    return (cos_real - direction * sin_imag, cos_imag + direction * sin_real)


def spectral_conv(gated, filters, my_index, tok_rows, count_ctx):
    chans = gated.shape[1]
    groups = filters.shape[1]
    share = chans // groups
    sub_rows = tok_rows // count_ctx
    period = 2 * count_ctx * tok_rows
    got_source, got_filter = (
        lax.all_to_all(
            gated.reshape(1, tok_rows, chans), "ctx", split_axis=1, concat_axis=0, tiled=True
        ),
        lax.all_to_all(
            filters.reshape(1, tok_rows, groups), "ctx", split_axis=1, concat_axis=0, tiled=True
        ),
    )
    coarse_idx = jnp.arange(count_ctx, dtype=jnp.int32)
    coarse_freq = jnp.arange(2 * count_ctx, dtype=jnp.int32)
    coarse_angle = angle_table(coarse_freq, coarse_idx, 2 * count_ctx)
    cos_coarse = jnp.cos(coarse_angle)
    sin_coarse = jnp.sin(coarse_angle)
    fine_global = my_index * sub_rows + jnp.arange(sub_rows, dtype=jnp.int32)
    twist_in = angle_table(coarse_freq, fine_global, period)
    source_re, source_im = section_coarse(
        got_source.astype(jnp.float32), cos_coarse, sin_coarse, twist_in
    )
    filter_re, filter_im = section_coarse(
        got_filter.astype(jnp.float32), cos_coarse, sin_coarse, twist_in
    )
    source_re, source_im, filter_re, filter_im = (
        lax.all_to_all(
            source_re.astype(jnp.bfloat16), "ctx", split_axis=0, concat_axis=1, tiled=True
        ).astype(source_re.dtype),
        lax.all_to_all(
            source_im.astype(jnp.bfloat16), "ctx", split_axis=0, concat_axis=1, tiled=True
        ).astype(source_im.dtype),
        lax.all_to_all(
            filter_re.astype(jnp.bfloat16), "ctx", split_axis=0, concat_axis=1, tiled=True
        ).astype(filter_re.dtype),
        lax.all_to_all(
            filter_im.astype(jnp.bfloat16), "ctx", split_axis=0, concat_axis=1, tiled=True
        ).astype(filter_im.dtype),
    )
    fine_idx = jnp.arange(tok_rows, dtype=jnp.int32)
    fine_angle = angle_table(fine_idx, fine_idx, tok_rows)
    cos_fine = jnp.cos(fine_angle)
    sin_fine = jnp.sin(fine_angle)
    source_re, source_im = section_fine(source_re, source_im, cos_fine, sin_fine, -1.0)
    filter_re, filter_im = section_fine(filter_re, filter_im, cos_fine, sin_fine, -1.0)
    split_re = source_re.reshape(2, tok_rows, groups, share)
    split_im = source_im.reshape(2, tok_rows, groups, share)
    prod_re = split_re * filter_re[..., None] - split_im * filter_im[..., None]
    prod_im = split_re * filter_im[..., None] + split_im * filter_re[..., None]
    back_re, back_im = section_fine(
        prod_re.reshape(2, tok_rows, chans),
        prod_im.reshape(2, tok_rows, chans),
        cos_fine,
        sin_fine,
        1.0,
    )
    pair_freq = my_index * 2 + jnp.arange(2, dtype=jnp.int32)
    twist_out = angle_table(pair_freq, fine_idx, period)
    cos_out = jnp.cos(twist_out)[:, :, None]
    sin_out = jnp.sin(twist_out)[:, :, None]
    turned_re = back_re * cos_out - back_im * sin_out
    turned_im = back_re * sin_out + back_im * cos_out
    turned_re, turned_im = (
        lax.all_to_all(
            turned_re.astype(jnp.bfloat16), "ctx", split_axis=1, concat_axis=0, tiled=True
        ).astype(turned_re.dtype),
        lax.all_to_all(
            turned_im.astype(jnp.bfloat16), "ctx", split_axis=1, concat_axis=0, tiled=True
        ).astype(turned_im.dtype),
    )
    result = jnp.einsum("nk,ksc->nsc", cos_coarse.T, turned_re, precision=highest)
    result = result - jnp.einsum("nk,ksc->nsc", sin_coarse.T, turned_im, precision=highest)
    rounded = (result / period).astype(jnp.bfloat16)
    returned = lax.all_to_all(rounded, "ctx", split_axis=0, concat_axis=1, tiled=True)
    return returned.reshape(tok_rows, chans)


def keep_same(running):
    return running


def attend_block(group_query, group_pos, key_block, value_block, key_pos, score_scale, group_state):
    run_max, run_total, run_accum = group_state
    scores = (
        jnp.einsum("thd,shd->hts", group_query, key_block, preferred_element_type=jnp.float32)
        * score_scale
    )
    allowed = (key_pos[None, :] <= group_pos[:, None])[None]
    block_max = jnp.max(jnp.where(allowed, scores, neg_large), axis=2)
    new_max = jnp.maximum(run_max, block_max)
    factor = jnp.exp(run_max - new_max)
    weights = jnp.where(allowed, jnp.exp(scores - new_max[:, :, None]), 0.0)
    new_total = run_total * factor + jnp.sum(weights, axis=2)
    new_accum = run_accum * factor[:, :, None] + jnp.einsum(
        "hts,shd->htd",
        weights.astype(jnp.bfloat16),
        value_block,
        preferred_element_type=jnp.float32,
    )
    return (new_max, new_total, new_accum)


def attention(q_attn, k_attn, v_attn, my_index, tok_rows):
    heads_local = q_attn.shape[1] // HD
    score_scale = HD ** (-0.5)
    queries = q_attn.reshape(tok_rows, heads_local, HD)
    group_list = [(queries, my_index * tok_rows + jnp.arange(tok_rows, dtype=jnp.int32))]
    initial = tuple(
        (
            (
                jnp.full((heads_local, entry[0].shape[0]), neg_large, jnp.float32),
                jnp.zeros((heads_local, entry[0].shape[0]), jnp.float32),
                jnp.zeros((heads_local, entry[0].shape[0], HD), jnp.float32),
            )
            for entry in group_list
        )
    )
    key_piece = lax.all_gather(k_attn, "ctx", axis=0, tiled=True)
    value_piece = lax.all_gather(v_attn, "ctx", axis=0, tiled=True)
    count_blocks = key_piece.shape[0] // tok_rows
    keys_split = key_piece.reshape(count_blocks, tok_rows, heads_local, HD)
    values_split = value_piece.reshape(count_blocks, tok_rows, heads_local, HD)

    def one_block(carry, item):
        key_block, value_block, block_number = item
        block_first = block_number * tok_rows
        key_pos = block_first + jnp.arange(tok_rows, dtype=jnp.int32)
        updated = []
        for entry, group_state in zip(group_list, carry):
            step_fn = partial(
                attend_block, entry[0], entry[1], key_block, value_block, key_pos, score_scale
            )
            updated.append(lax.cond(block_first <= entry[1][-1], step_fn, keep_same, group_state))
        return (tuple(updated), None)

    new_state, unused = lax.scan(
        one_block, initial, (keys_split, values_split, jnp.arange(count_blocks, dtype=jnp.int32))
    )
    outputs = [
        (state[2] / state[1][:, :, None]).transpose(1, 0, 2).astype(jnp.bfloat16)
        for state in new_state
    ]
    merged = outputs[0]
    return merged.reshape(tok_rows, heads_local * HD)


def local(q_conv, k_conv, v_conv, conv_filter, q_attn, k_attn, v_attn, w_conv_out, w_attn_out):
    count_ctx = lax.axis_size("ctx")
    my_index = lax.axis_index("ctx")
    tok_rows = q_conv.shape[0]
    gated = (k_conv.astype(jnp.float32) * v_conv.astype(jnp.float32)).astype(jnp.bfloat16)
    conv = spectral_conv(gated, conv_filter, my_index, tok_rows, count_ctx)
    mixed = (q_conv.astype(jnp.float32) * conv.astype(jnp.float32)).astype(jnp.bfloat16)
    attended = attention(q_attn, k_attn, v_attn, my_index, tok_rows)
    return lax.psum_scatter(
        (
            jnp.dot(mixed, w_conv_out, preferred_element_type=jnp.float32)
            + jnp.dot(attended, w_attn_out, preferred_element_type=jnp.float32)
        ).astype(jnp.bfloat16),
        "ch",
        scatter_dimension=0,
        tiled=True,
    )


def solution(mesh):
    return jax.shard_map(
        local,
        mesh=mesh,
        in_specs=(
            P("ctx", "ch"),
            P("ctx", "ch"),
            P("ctx", "ch"),
            P("ctx", "ch"),
            P("ctx", "ch"),
            P("ctx", "ch"),
            P("ctx", "ch"),
            P("ch", None),
            P("ch", None),
        ),
        out_specs=P(("ctx", "ch"), None),
        check_vma=False,
    )
```

profile of v0, /device:TPU:1, one launch (start us, length us, event | category | flops | bytes accessed | tf_op | source)
XLA Modules:
  0.0 611.6 jit_solution(7817200553837334792)
XLA Ops:
  11.1 11.3 %all-to-all-start.3 = ((bf16[32,2,224]{2,1,0:T(2,128)(2,1)}), bf16[32,2,224]{2,1,0:T(2,128)(2,1)S(1)}, u32[]{:S(2)}, u32[]{:S(2)}) async-start(bf16[32,2,224]{2,1,0:T(2,128)(2,1)} %reshape.188), calls=%async_computation.3 | async-start | bytes 65536 | tf_op jit(solution)/shard_map/all_to_all | solution.py:48
  31.3 7.0 %all-to-all-start = ((bf16[32,2,3584]{2,1,0:T(2,128)(2,1)}), bf16[32,2,3584]{2,1,0:T(2,128)(2,1)S(1)}, u32[]{:S(2)}, u32[]{:S(2)}) async-start(bf16[32,2,3584]{2,1,0:T(2,128)(2,1)} %reshape.194), calls=%async_computation | async-start | bytes 917504 | tf_op jit(solution)/shard_map/all_to_all | solution.py:45
  41.2 7.5 %all-to-all-done = bf16[32,2,3584]{2,1,0:T(2,128)(2,1)S(1)} async-done(((bf16[32,2,3584]{2,1,0:T(2,128)(2,1)}), bf16[32,2,3584]{2,1,0:T(2,128)(2,1)S(1)}, u32[]{:S(2)}, u32[]{:S(2)}) %all-to-all-start) | async-done | bytes 458784 | tf_op jit(solution)/shard_map/all_to_all | solution.py:45
  48.7 4.4 all-to-all-start.5
  57.7 5.0 all-to-all-done.5
  62.7 4.3 all-to-all-start.4
  71.2 5.3 all-to-all-done.4
  83.0 19.3 %all-to-all-done.1 = bf16[64,7,1024]{2,1,0:T(8,128)(2,1)S(1)} async-done(((bf16[64,7,1024]{2,1,0:T(8,128)(2,1)}), bf16[64,7,1024]{2,1,0:T(8,128)(2,1)S(1)}, u32[]{:S(2)}, u32[]{:S(2)}) %all-to-all-start.1) | async-done | bytes 917536 | tf_op jit(solution)/shard_map/all_to_all | solution.py:66
  102.2 5.0 all-to-all-start.2
  118.6 6.3 %all-to-all-done.2 = bf16[64,7,1024]{2,1,0:T(8,128)(2,1)} async-done(((bf16[64,7,1024]{2,1,0:T(8,128)(2,1)}), bf16[64,7,1024]{2,1,0:T(8,128)(2,1)}, u32[]{:S(2)}, u32[]{:S(2)}) %all-to-all-start.2) | async-done | bytes 917536 | tf_op jit(solution)/shard_map/all_to_all | solution.py:69
  155.4 10.4 %all-to-all-done.7 = bf16[2,224,1024]{2,0,1:T(2,128)(2,1)S(1)} async-done(((bf16[2,224,1024]{2,0,1:T(2,128)(2,1)}), bf16[2,224,1024]{2,0,1:T(2,128)(2,1)S(1)}, u32[]{:S(2)}, u32[]{:S(2)}) %all-to-all-start.7) | async-done | bytes 917536 | tf_op jit(solution)/shard_map/all_to_all | solution.py:106
  165.8 6.0 all-to-all-start.6
  172.7 19.2 %all-to-all-done.6 = bf16[2,224,1024]{2,0,1:T(2,128)(2,1)S(1)} async-done(((bf16[2,224,1024]{2,0,1:T(2,128)(2,1)}), bf16[2,224,1024]{2,0,1:T(2,128)(2,1)S(1)}, u32[]{:S(2)}, u32[]{:S(2)}) %all-to-all-start.6) | async-done | bytes 917536 | tf_op jit(solution)/shard_map/all_to_all | solution.py:103
  195.3 5.5 all-to-all-start.8
  201.0 10.9 %all-to-all-done.8 = bf16[32,7,1024]{2,1,0:T(8,128)(2,1)S(1)} async-done(((bf16[32,7,1024]{2,1,0:T(8,128)(2,1)}), bf16[32,7,1024]{2,1,0:T(8,128)(2,1)S(1)}, u32[]{:S(2)}, u32[]{:S(2)}) %all-to-all-start.8) | async-done | bytes 458784 | tf_op jit(solution)/shard_map/all_to_all | solution.py:113
  212.0 7.3 %fusion.37 = f32[224,4096]{1,0:T(8,128)} fusion(bf16[1024,4096]{1,0:T(8,128)(2,1)} %param.20, f32[224,1024]{1,0:T(8,128)S(1)} %reshape.181, bf16[224,1024]{1,0:T(8,128)(2,1)S(1)} %copy-done.6), kind=kOutput, calls=%fused_computation.63 | convolution fusion | flops 1879736320 | bytes 13434880 | tf_op jit(solution)/shard_map/dot_general | solution.py:196
  219.3 9.2 %copy.126 = bf16[896,8,8,128]{3,2,1,0:T(8,128)(2,1)S(1)} copy(bf16[896,8,8,128]{3,1,2,0:T(8,128)(2,1)} %bitcast.171) | data formatting | bytes 29360128
  228.6 7.3 %copy.117 = bf16[32,224,8,128]{3,1,2,0:T(8,128)(2,1)} copy(bf16[32,224,8,128]{3,2,1,0:T(8,128)(2,1)S(1)} %bitcast.169) | data formatting | bytes 29360128 | tf_op jit(solution)/shard_map/while | solution.py:175
  235.9 97.1 %all-gather.5.cloned.1.call-done = bf16[7168,1024]{1,0:T(8,128)(2,1)} async-done(((bf16[224,1024]{1,0:T(8,128)(2,1)}), bf16[7168,1024]{1,0:T(8,128)(2,1)}) %all-gather.5.cloned.1.call-update) | async-done | bytes 14680080 | tf_op jit(solution)/shard_map/all_gather | solution.py:158
  333.0 9.1 %copy.127 = bf16[896,8,8,128]{3,2,1,0:T(8,128)(2,1)S(1)} copy(bf16[896,8,8,128]{3,1,2,0:T(8,128)(2,1)} %bitcast.172) | data formatting | bytes 29360128
  342.1 7.3 %copy.119 = bf16[32,224,8,128]{3,1,2,0:T(8,128)(2,1)} copy(bf16[32,224,8,128]{3,2,1,0:T(8,128)(2,1)S(1)} %bitcast.170) | data formatting | bytes 29360128 | tf_op jit(solution)/shard_map/while | solution.py:175
  349.5 92.0 %while.14 = (s32[]{:T(128)}, f32[8,224]{1,0:T(8,128)S(1)}, f32[8,224]{1,0:T(8,128)S(1)}, f32[8,224,128]{2,1,0:T(8,128)S(1)}, s32[32]{0:T(128)S(1)}, /*index=5*/s...) while((s32[]{:T(128)}, f32[8,224]{1,0:T(8,128)S(1)}, ...), condition=%wide.region_5.6_spmd, body=%wide.region_0.5_spmd.sunk | while | flops 210449120 | bytes 8349359 | solution.py:175
  441.5 7.9 %fusion.19 = bf16[224,4096]{1,0:T(8,128)(2,1)} fusion(f32[224,4096]{1,0:T(8,128)} %fusion.37, bf16[1024,4096]{1,0:T(8,128)(2,1)} %param.21, f32[8,224,128]{2,1,0:T(8,128)S(1)} %get-tuple-element.145, f32[8,224]{1,0:T(8,128)S(1)} %get-tuple-element.146), kind=kOutput, calls=%fused_computation.26 | convolution fusion | flops 1881341952 | bytes 14818304 | tf_op jit(solution)/shard_map/dot_general | solution.py:197
  449.4 155.4 %reduce-scatter.2.cloned.1.call-done = bf16[56,4096]{1,0:T(8,128)(2,1)} async-done(((bf16[224,4096]{1,0:T(8,128)(2,1)}), bf16[56,4096]{1,0:T(8,128)(2,1)}) %reduce-scatter.2.cloned.1.call-update) | async-done | bytes 458768 | tf_op jit(solution)/shard_map/reduce_scatter | solution.py:194
  (228 shorter events, 128.7 us)
Async XLA Ops:
  6.5 194.3 %copy-start = (bf16[224,1024]{1,0:T(8,128)(2,1)S(1)}, bf16[224,1024]{1,0:T(8,128)(2,1)}, u32[]{:S(2)}) copy-start(bf16[224,1024]{1,0:T(8,128)(2,1)} %param.17) | copy-start | bytes 1376260
  6.5 212.8 %all-gather.3.cloned.1.call-start = ((), (), s32[]{:S(2)}) async-start(), calls=%async_computation.10 | async-start | bytes 15138816 | tf_op jit(solution)/shard_map/all_gather | solution.py:157
  7.3 325.7 %all-gather.5.cloned.1.call-start = ((), (), s32[]{:S(2)}) async-start(), calls=%async_computation.11 | async-start | bytes 15138816 | tf_op jit(solution)/shard_map/all_gather | solution.py:158
  11.1 20.2 %all-to-all-start.3 = ((bf16[32,2,224]{2,1,0:T(2,128)(2,1)}), bf16[32,2,224]{2,1,0:T(2,128)(2,1)S(1)}, u32[]{:S(2)}, u32[]{:S(2)}) async-start(bf16[32,2,224]{2,1,0:T(2,128)(2,1)} %reshape.188), calls=%async_computation.3 | async-start | bytes 65536 | tf_op jit(solution)/shard_map/all_to_all | solution.py:48
  31.3 17.5 %all-to-all-start = ((bf16[32,2,3584]{2,1,0:T(2,128)(2,1)}), bf16[32,2,3584]{2,1,0:T(2,128)(2,1)S(1)}, u32[]{:S(2)}, u32[]{:S(2)}) async-start(bf16[32,2,3584]{2,1,0:T(2,128)(2,1)} %reshape.194), calls=%async_computation | async-start | bytes 917504 | tf_op jit(solution)/shard_map/all_to_all | solution.py:45
  48.7 14.0 %all-to-all-start.5 = ((bf16[32,2,448]{2,1,0:T(2,128)(2,1)}), bf16[32,2,448]{2,1,0:T(2,128)(2,1)S(1)}, u32[]{:S(2)}, u32[]{:S(2)}) async-start(bf16[32,2,448]{2,1,0:T(2,128)(2,1)} %reshape.192), calls=%async_computation.5 | async-start | bytes 131072 | tf_op jit(solution)/shard_map/all_to_all | solution.py:75
  62.7 13.8 %all-to-all-start.4 = ((bf16[32,2,448]{2,1,0:T(2,128)(2,1)}), bf16[32,2,448]{2,1,0:T(2,128)(2,1)S(1)}, u32[]{:S(2)}, u32[]{:S(2)}) async-start(bf16[32,2,448]{2,1,0:T(2,128)(2,1)} %reshape.190), calls=%async_computation.4 | async-start | bytes 131072 | tf_op jit(solution)/shard_map/all_to_all | solution.py:72
  71.2 10.2 %copy-start.5 = (bf16[64,7,1024]{2,0,1:T(8,128)(2,1)S(1)}, bf16[64,7,1024]{2,0,1:T(8,128)(2,1)}, u32[]{:S(2)}) copy-start(bf16[64,7,1024]{2,0,1:T(8,128)(2,1)} %get-tuple-element.199) | copy-start | bytes 2752516
  76.5 25.7 %all-to-all-start.1 = ((bf16[64,7,1024]{2,1,0:T(8,128)(2,1)}), bf16[64,7,1024]{2,1,0:T(8,128)(2,1)S(1)}, u32[]{:S(2)}, u32[]{:S(2)}) async-start(bf16[64,7,1024]{2,1,0:T(8,128)(2,1)} %copy.89), calls=%async_computation.1 | async-start | bytes 2097152 | tf_op jit(solution)/shard_map/all_to_all | solution.py:66
  102.2 6.2 %copy-start.4 = (bf16[64,7,1024]{2,1,0:T(8,128)(2,1)}, bf16[64,7,1024]{2,1,0:T(8,128)(2,1)S(1)}, u32[]{:S(2)}) copy-start(bf16[64,7,1024]{2,1,0:T(8,128)(2,1)S(1)} %all-to-all-done.1) | copy-start | bytes 2752516
  102.2 22.6 %all-to-all-start.2 = ((bf16[64,7,1024]{2,1,0:T(8,128)(2,1)}), bf16[64,7,1024]{2,1,0:T(8,128)(2,1)}, u32[]{:S(2)}, u32[]{:S(2)}) async-start(bf16[64,7,1024]{2,1,0:T(8,128)(2,1)} %copy.92), calls=%async_computation.2 | async-start | bytes 2097152 | tf_op jit(solution)/shard_map/all_to_all | solution.py:69
  130.8 2.0 copy-start.2
  130.8 2.0 copy-start.3
  149.3 16.5 %all-to-all-start.7 = ((bf16[2,224,1024]{2,0,1:T(2,128)(2,1)}), bf16[2,224,1024]{2,0,1:T(2,128)(2,1)S(1)}, u32[]{:S(2)}, u32[]{:S(2)}) async-start(bf16[2,224,1024]{2,0,1:T(2,128)(2,1)} %copy.114), calls=%async_computation.7 | async-start | bytes 1835008 | tf_op jit(solution)/shard_map/all_to_all | solution.py:106
  165.8 26.2 %all-to-all-start.6 = ((bf16[2,224,1024]{2,0,1:T(2,128)(2,1)}), bf16[2,224,1024]{2,0,1:T(2,128)(2,1)S(1)}, u32[]{:S(2)}, u32[]{:S(2)}) async-start(bf16[2,224,1024]{2,0,1:T(2,128)(2,1)} %copy.112), calls=%async_computation.6 | async-start | bytes 1835008 | tf_op jit(solution)/shard_map/all_to_all | solution.py:103
  195.3 16.7 %copy-start.6 = (bf16[224,1024]{1,0:T(8,128)(2,1)S(1)}, bf16[224,1024]{1,0:T(8,128)(2,1)}, u32[]{:S(2)}) copy-start(bf16[224,1024]{1,0:T(8,128)(2,1)} %param.13) | copy-start | bytes 1376260
  195.3 16.6 %all-to-all-start.8 = ((bf16[32,7,1024]{2,1,0:T(8,128)(2,1)}), bf16[32,7,1024]{2,1,0:T(8,128)(2,1)S(1)}, u32[]{:S(2)}, u32[]{:S(2)}) async-start(bf16[32,7,1024]{2,1,0:T(8,128)(2,1)} %copy.116), calls=%async_computation.8 | async-start | bytes 1048576 | tf_op jit(solution)/shard_map/all_to_all | solution.py:113
  200.8 404.0 %reduce-scatter.2.cloned.1.call-start = ((), (), s32[]{:S(2)}) async-start(), calls=%async_computation.12 | async-start | bytes 2293760 | tf_op jit(solution)/shard_map/reduce_scatter | solution.py:194
  441.5 163.3 %copy-start.1 = (bf16[224,1024]{1,0:T(8,128)(2,1)S(1)}, bf16[224,1024]{1,0:T(8,128)(2,1)}, u32[]{:S(2)}) copy-start(bf16[224,1024]{1,0:T(8,128)(2,1)} %param.17) | copy-start | bytes 1376260
Sparse Core Ops, SparseCore 0:
  10.4 179.5 all-gather.2
  193.1 139.8 all-gather.4
  449.5 155.2 reduce-scatter.1
where the time goes:
time: 622 us; the launch traced here: 612 us
  waiting for transfers between devices  340 us (55%)
  local copies, waits for them, and re-layouts  104 us (17%)
  starting transfers between devices  51.9 us (8%)
  matrix products  49.7 us (8%)
  loops' own time  45.7 us (7%)
  between operations  13.9 us (2%)
  other arithmetic  6.44 us (1%)
    reduce_scatter x1, waiting for transfers between devices, local(): lax.psum_scatter((jnp.dot(mixed, w_conv_out, preferred_element_type=jnp.f...  155 us
    all_gather x1, waiting for transfers between devices, attention(): value_piece = lax.all_gather(v_attn, 'ctx', axis=0, tiled=True)  97.1 us
    another operation x1, loops' own time, attention(): lax.scan(one_block, initial, (keys_split, values_split, jnp.arange(count_...  45.1 us
    unnamed x25, local copies, waits for them, and re-layouts  23 us
    dynamic_slice x32, local copies, waits for them, and re-layouts, attention(): lax.scan(one_block, initial, (keys_split, values_split, jnp.arange(count_...  21.2 us
    slice x32, local copies, waits for them, and re-layouts, one_block(): entry[1][-1]  20.8 us
    all_to_all x1, waiting for transfers between devices, spectral_conv(): lax.all_to_all(source_re.astype(jnp.bfloat16), 'ctx', split_axis=0, conca...  19.3 us
    all_to_all x1, waiting for transfers between devices, spectral_conv(): lax.all_to_all(turned_re.astype(jnp.bfloat16), 'ctx', split_axis=1, conca...  19.2 us
  transfers between devices with their start and end apart: 12, of which 11 were waited for; matrix products, arithmetic and copies ran while one was open for 14% of the time, Pallas kernels for 0%

commit v1 on v0

--- a/solution.py
+++ b/solution.py
@@ -9,6 +9,13 @@
 two_pi = 2.0 * math.pi
 neg_large = -1e30
 highest = lax.Precision.HIGHEST
+
+
+def exchange_blocks(x, axis, split, join):
+    peers = lax.axis_size(axis)
+    tiles = jnp.stack(jnp.split(x, peers, axis=split), axis=0)
+    tiles = lax.all_to_all(tiles, axis, split_axis=0, concat_axis=0)
+    return jnp.concatenate(tiles, axis=join)
 
 
 def angle_table(left_idx, right_idx, period):
@@ -100,9 +107,7 @@
     turned_re = back_re * cos_out - back_im * sin_out
     turned_im = back_re * sin_out + back_im * cos_out
     turned_re, turned_im = (
-        lax.all_to_all(
-            turned_re.astype(jnp.bfloat16), "ctx", split_axis=1, concat_axis=0, tiled=True
-        ).astype(turned_re.dtype),
+        exchange_blocks(turned_re.astype(jnp.bfloat16), "ctx", 1, 0).astype(turned_re.dtype),
         lax.all_to_all(
             turned_im.astype(jnp.bfloat16), "ctx", split_axis=1, concat_axis=0, tiled=True
         ).astype(turned_im.dtype),

time: 622 us -> 622 us (level)
    unnamed x25 -> x56, local copies, waits for them, and re-layouts: 23 us -> 23.4 us
  transfers between devices with their start and end apart: 12 -> 12, of which waited for: 11 -> 11; matrix products, arithmetic and copies ran while one was open for 14% -> 15% of each run, Pallas kernels for 0% -> 0%
where the time goes in v1:
time: 622 us; the launch traced here: 611 us
  waiting for transfers between devices  339 us (55%)
  local copies, waits for them, and re-layouts  105 us (17%)
  starting transfers between devices  51.9 us (8%)
  matrix products  49.7 us (8%)
  loops' own time  45.6 us (7%)
  between operations  14.1 us (2%)
  other arithmetic  6.44 us (1%)
    reduce_scatter x1, waiting for transfers between devices, local(): lax.psum_scatter((jnp.dot(mixed, w_conv_out, preferred_element_type=jnp.f...  155 us
    all_gather x1, waiting for transfers between devices, attention(): value_piece = lax.all_gather(v_attn, 'ctx', axis=0, tiled=True)  97.1 us
    another operation x1, loops' own time, attention(): lax.scan(one_block, initial, (keys_split, values_split, jnp.arange(count_...  45.1 us
    unnamed x56, local copies, waits for them, and re-layouts  23.4 us
    dynamic_slice x32, local copies, waits for them, and re-layouts, attention(): lax.scan(one_block, initial, (keys_split, values_split, jnp.arange(count_...  21.2 us
    slice x32, local copies, waits for them, and re-layouts, one_block(): entry[1][-1]  20.8 us
    all_to_all x1, waiting for transfers between devices, spectral_conv(): lax.all_to_all(source_re.astype(jnp.bfloat16), 'ctx', split_axis=0, conca...  19.3 us
    all_to_all x1, waiting for transfers between devices, exchange_blocks(): tiles = lax.all_to_all(tiles, axis, split_axis=0, concat_axis=0)  19.2 us
  transfers between devices with their start and end apart: 12, of which 11 were waited for; matrix products, arithmetic and copies ran while one was open for 15% of the time, Pallas kernels for 0%

profile of v1, /device:TPU:1, one launch (start us, length us, event | category | flops | bytes accessed | tf_op | source)
XLA Modules:
  0.0 611.2 jit_solution(16669863039959866312)
XLA Ops:
  11.1 11.3 %all-to-all-start.3 = ((bf16[32,2,224]{2,1,0:T(2,128)(2,1)}), bf16[32,2,224]{2,1,0:T(2,128)(2,1)S(1)}, u32[]{:S(2)}, u32[]{:S(2)}) async-start(bf16[32,2,224]{2,1,0:T(2,128)(2,1)} %reshape.192), calls=%async_computation.3 | async-start | bytes 65536 | tf_op jit(solution)/shard_map/all_to_all | solution.py:55
  31.3 7.0 %all-to-all-start = ((bf16[32,2,3584]{2,1,0:T(2,128)(2,1)}), bf16[32,2,3584]{2,1,0:T(2,128)(2,1)S(1)}, u32[]{:S(2)}, u32[]{:S(2)}) async-start(bf16[32,2,3584]{2,1,0:T(2,128)(2,1)} %reshape.198), calls=%async_computation | async-start | bytes 917504 | tf_op jit(solution)/shard_map/all_to_all | solution.py:52
  41.2 7.5 %all-to-all-done = bf16[32,2,3584]{2,1,0:T(2,128)(2,1)S(1)} async-done(((bf16[32,2,3584]{2,1,0:T(2,128)(2,1)}), bf16[32,2,3584]{2,1,0:T(2,128)(2,1)S(1)}, u32[]{:S(2)}, u32[]{:S(2)}) %all-to-all-start) | async-done | bytes 458784 | tf_op jit(solution)/shard_map/all_to_all | solution.py:52
  48.7 4.4 all-to-all-start.5
  57.7 5.0 all-to-all-done.5
  62.7 4.3 all-to-all-start.4
  71.2 5.3 all-to-all-done.4
  83.0 19.3 %all-to-all-done.1 = bf16[64,7,1024]{2,1,0:T(8,128)(2,1)S(1)} async-done(((bf16[64,7,1024]{2,1,0:T(8,128)(2,1)}), bf16[64,7,1024]{2,1,0:T(8,128)(2,1)S(1)}, u32[]{:S(2)}, u32[]{:S(2)}) %all-to-all-start.1) | async-done | bytes 917536 | tf_op jit(solution)/shard_map/all_to_all | solution.py:73
  102.2 5.0 all-to-all-start.2
  118.6 6.3 %all-to-all-done.2 = bf16[64,7,1024]{2,1,0:T(8,128)(2,1)} async-done(((bf16[64,7,1024]{2,1,0:T(8,128)(2,1)}), bf16[64,7,1024]{2,1,0:T(8,128)(2,1)}, u32[]{:S(2)}, u32[]{:S(2)}) %all-to-all-start.2) | async-done | bytes 917536 | tf_op jit(solution)/shard_map/all_to_all | solution.py:76
  156.2 9.6 %all-to-all-done.7 = bf16[2,224,1024]{2,0,1:T(2,128)(2,1)S(1)} async-done(((bf16[2,224,1024]{2,0,1:T(2,128)(2,1)}), bf16[2,224,1024]{2,0,1:T(2,128)(2,1)S(1)}, u32[]{:S(2)}, u32[]{:S(2)}) %all-to-all-start.7) | async-done | bytes 917536 | tf_op jit(solution)/shard_map/all_to_all | solution.py:111
  165.8 6.0 all-to-all-start.6
  172.7 19.2 %all-to-all-done.6 = bf16[32,2,7,1024]{3,1,2,0:T(2,128)(2,1)S(1)} async-done(((bf16[32,2,7,1024]{3,1,2,0:T(2,128)(2,1)}), bf16[32,2,7,1024]{3,1,2,0:T(2,128)(2,1)S(1)}, u32[]{:S(2)}, u32[]{:S(2)}) %all-to-all-start.6) | async-done | bytes 917536 | tf_op jit(solution)/shard_map/all_to_all | solution.py:17
  195.3 5.5 all-to-all-start.8
  201.0 10.9 %all-to-all-done.8 = bf16[32,7,1024]{2,1,0:T(8,128)(2,1)S(1)} async-done(((bf16[32,7,1024]{2,1,0:T(8,128)(2,1)}), bf16[32,7,1024]{2,1,0:T(8,128)(2,1)S(1)}, u32[]{:S(2)}, u32[]{:S(2)}) %all-to-all-start.8) | async-done | bytes 458784 | tf_op jit(solution)/shard_map/all_to_all | solution.py:118
  212.0 7.3 %fusion.37 = f32[224,4096]{1,0:T(8,128)} fusion(bf16[1024,4096]{1,0:T(8,128)(2,1)} %param.20, f32[224,1024]{1,0:T(8,128)S(1)} %reshape.185, bf16[224,1024]{1,0:T(8,128)(2,1)S(1)} %copy-done.6), kind=kOutput, calls=%fused_computation.63 | convolution fusion | flops 1879736320 | bytes 13434880 | tf_op jit(solution)/shard_map/dot_general | solution.py:201
  219.3 9.2 %copy.125 = bf16[896,8,8,128]{3,2,1,0:T(8,128)(2,1)S(1)} copy(bf16[896,8,8,128]{3,1,2,0:T(8,128)(2,1)} %bitcast.296) | data formatting | bytes 29360128
  228.6 7.3 %copy.116 = bf16[32,224,8,128]{3,1,2,0:T(8,128)(2,1)} copy(bf16[32,224,8,128]{3,2,1,0:T(8,128)(2,1)S(1)} %bitcast.294) | data formatting | bytes 29360128 | tf_op jit(solution)/shard_map/while | solution.py:180
  235.9 97.1 %all-gather.5.cloned.1.call-done = bf16[7168,1024]{1,0:T(8,128)(2,1)} async-done(((bf16[224,1024]{1,0:T(8,128)(2,1)}), bf16[7168,1024]{1,0:T(8,128)(2,1)}) %all-gather.5.cloned.1.call-update) | async-done | bytes 14680080 | tf_op jit(solution)/shard_map/all_gather | solution.py:163
  333.0 9.1 %copy.126 = bf16[896,8,8,128]{3,2,1,0:T(8,128)(2,1)S(1)} copy(bf16[896,8,8,128]{3,1,2,0:T(8,128)(2,1)} %bitcast.297) | data formatting | bytes 29360128
  342.1 7.3 %copy.118 = bf16[32,224,8,128]{3,1,2,0:T(8,128)(2,1)} copy(bf16[32,224,8,128]{3,2,1,0:T(8,128)(2,1)S(1)} %bitcast.295) | data formatting | bytes 29360128 | tf_op jit(solution)/shard_map/while | solution.py:180
  349.5 91.9 %while.14 = (s32[]{:T(128)}, f32[8,224]{1,0:T(8,128)S(1)}, f32[8,224]{1,0:T(8,128)S(1)}, f32[8,224,128]{2,1,0:T(8,128)S(1)}, s32[32]{0:T(128)S(1)}, /*index=5*/s...) while((s32[]{:T(128)}, f32[8,224]{1,0:T(8,128)S(1)}, ...), condition=%wide.region_5.6_spmd, body=%wide.region_0.5_spmd.sunk | while | flops 210449120 | bytes 8349359 | solution.py:180
  441.4 7.9 %fusion.19 = bf16[224,4096]{1,0:T(8,128)(2,1)} fusion(f32[224,4096]{1,0:T(8,128)} %fusion.37, bf16[1024,4096]{1,0:T(8,128)(2,1)} %param.21, f32[8,224,128]{2,1,0:T(8,128)S(1)} %get-tuple-element.145, f32[8,224]{1,0:T(8,128)S(1)} %get-tuple-element.146), kind=kOutput, calls=%fused_computation.26 | convolution fusion | flops 1881341952 | bytes 14818304 | tf_op jit(solution)/shard_map/dot_general | solution.py:202
  449.3 155.1 %reduce-scatter.2.cloned.1.call-done = bf16[56,4096]{1,0:T(8,128)(2,1)} async-done(((bf16[224,4096]{1,0:T(8,128)(2,1)}), bf16[56,4096]{1,0:T(8,128)(2,1)}) %reduce-scatter.2.cloned.1.call-update) | async-done | bytes 458768 | tf_op jit(solution)/shard_map/reduce_scatter | solution.py:199
  (260 shorter events, 129.2 us)
Async XLA Ops:
  6.5 194.3 %copy-start = (bf16[224,1024]{1,0:T(8,128)(2,1)S(1)}, bf16[224,1024]{1,0:T(8,128)(2,1)}, u32[]{:S(2)}) copy-start(bf16[224,1024]{1,0:T(8,128)(2,1)} %param.17) | copy-start | bytes 1376260
  6.5 212.8 %all-gather.3.cloned.1.call-start = ((), (), s32[]{:S(2)}) async-start(), calls=%async_computation.10 | async-start | bytes 15138816 | tf_op jit(solution)/shard_map/all_gather | solution.py:162
  7.3 325.7 %all-gather.5.cloned.1.call-start = ((), (), s32[]{:S(2)}) async-start(), calls=%async_computation.11 | async-start | bytes 15138816 | tf_op jit(solution)/shard_map/all_gather | solution.py:163
  11.1 20.2 %all-to-all-start.3 = ((bf16[32,2,224]{2,1,0:T(2,128)(2,1)}), bf16[32,2,224]{2,1,0:T(2,128)(2,1)S(1)}, u32[]{:S(2)}, u32[]{:S(2)}) async-start(bf16[32,2,224]{2,1,0:T(2,128)(2,1)} %reshape.192), calls=%async_computation.3 | async-start | bytes 65536 | tf_op jit(solution)/shard_map/all_to_all | solution.py:55
  31.3 17.5 %all-to-all-start = ((bf16[32,2,3584]{2,1,0:T(2,128)(2,1)}), bf16[32,2,3584]{2,1,0:T(2,128)(2,1)S(1)}, u32[]{:S(2)}, u32[]{:S(2)}) async-start(bf16[32,2,3584]{2,1,0:T(2,128)(2,1)} %reshape.198), calls=%async_computation | async-start | bytes 917504 | tf_op jit(solution)/shard_map/all_to_all | solution.py:52
  48.7 14.0 %all-to-all-start.5 = ((bf16[32,2,448]{2,1,0:T(2,128)(2,1)}), bf16[32,2,448]{2,1,0:T(2,128)(2,1)S(1)}, u32[]{:S(2)}, u32[]{:S(2)}) async-start(bf16[32,2,448]{2,1,0:T(2,128)(2,1)} %reshape.196), calls=%async_computation.5 | async-start | bytes 131072 | tf_op jit(solution)/shard_map/all_to_all | solution.py:82
  62.7 13.8 %all-to-all-start.4 = ((bf16[32,2,448]{2,1,0:T(2,128)(2,1)}), bf16[32,2,448]{2,1,0:T(2,128)(2,1)S(1)}, u32[]{:S(2)}, u32[]{:S(2)}) async-start(bf16[32,2,448]{2,1,0:T(2,128)(2,1)} %reshape.194), calls=%async_computation.4 | async-start | bytes 131072 | tf_op jit(solution)/shard_map/all_to_all | solution.py:79
  71.2 10.2 %copy-start.5 = (bf16[64,7,1024]{2,0,1:T(8,128)(2,1)S(1)}, bf16[64,7,1024]{2,0,1:T(8,128)(2,1)}, u32[]{:S(2)}) copy-start(bf16[64,7,1024]{2,0,1:T(8,128)(2,1)} %get-tuple-element.199) | copy-start | bytes 2752516
  76.5 25.7 %all-to-all-start.1 = ((bf16[64,7,1024]{2,1,0:T(8,128)(2,1)}), bf16[64,7,1024]{2,1,0:T(8,128)(2,1)S(1)}, u32[]{:S(2)}, u32[]{:S(2)}) async-start(bf16[64,7,1024]{2,1,0:T(8,128)(2,1)} %copy.88), calls=%async_computation.1 | async-start | bytes 2097152 | tf_op jit(solution)/shard_map/all_to_all | solution.py:73
  102.2 6.2 %copy-start.4 = (bf16[64,7,1024]{2,1,0:T(8,128)(2,1)}, bf16[64,7,1024]{2,1,0:T(8,128)(2,1)S(1)}, u32[]{:S(2)}) copy-start(bf16[64,7,1024]{2,1,0:T(8,128)(2,1)S(1)} %all-to-all-done.1) | copy-start | bytes 2752516
  102.2 22.6 %all-to-all-start.2 = ((bf16[64,7,1024]{2,1,0:T(8,128)(2,1)}), bf16[64,7,1024]{2,1,0:T(8,128)(2,1)}, u32[]{:S(2)}, u32[]{:S(2)}) async-start(bf16[64,7,1024]{2,1,0:T(8,128)(2,1)} %copy.91), calls=%async_computation.2 | async-start | bytes 2097152 | tf_op jit(solution)/shard_map/all_to_all | solution.py:76
  130.8 2.0 copy-start.2
  130.8 2.0 copy-start.3
  149.3 16.5 %all-to-all-start.7 = ((bf16[2,224,1024]{2,0,1:T(2,128)(2,1)}), bf16[2,224,1024]{2,0,1:T(2,128)(2,1)S(1)}, u32[]{:S(2)}, u32[]{:S(2)}) async-start(bf16[2,224,1024]{2,0,1:T(2,128)(2,1)} %copy.113), calls=%async_computation.7 | async-start | bytes 1835008 | tf_op jit(solution)/shard_map/all_to_all | solution.py:111
  165.8 26.2 %all-to-all-start.6 = ((bf16[32,2,7,1024]{3,1,2,0:T(2,128)(2,1)}), bf16[32,2,7,1024]{3,1,2,0:T(2,128)(2,1)S(1)}, u32[]{:S(2)}, u32[]{:S(2)}) async-start(bf16[32,2,7,1024]{3,1,2,0:T(2,128)(2,1)} %copy.111), calls=%async_computation.6 | async-start | bytes 1835008 | tf_op jit(solution)/shard_map/all_to_all | solution.py:17
  195.3 16.7 %copy-start.6 = (bf16[224,1024]{1,0:T(8,128)(2,1)S(1)}, bf16[224,1024]{1,0:T(8,128)(2,1)}, u32[]{:S(2)}) copy-start(bf16[224,1024]{1,0:T(8,128)(2,1)} %param.13) | copy-start | bytes 1376260
  195.3 16.6 %all-to-all-start.8 = ((bf16[32,7,1024]{2,1,0:T(8,128)(2,1)}), bf16[32,7,1024]{2,1,0:T(8,128)(2,1)S(1)}, u32[]{:S(2)}, u32[]{:S(2)}) async-start(bf16[32,7,1024]{2,1,0:T(8,128)(2,1)} %copy.115), calls=%async_computation.8 | async-start | bytes 1048576 | tf_op jit(solution)/shard_map/all_to_all | solution.py:118
  200.8 403.7 %reduce-scatter.2.cloned.1.call-start = ((), (), s32[]{:S(2)}) async-start(), calls=%async_computation.12 | async-start | bytes 2293760 | tf_op jit(solution)/shard_map/reduce_scatter | solution.py:199
  441.4 163.0 %copy-start.1 = (bf16[224,1024]{1,0:T(8,128)(2,1)S(1)}, bf16[224,1024]{1,0:T(8,128)(2,1)}, u32[]{:S(2)}) copy-start(bf16[224,1024]{1,0:T(8,128)(2,1)} %param.17) | copy-start | bytes 1376260
Sparse Core Ops, SparseCore 0:
  10.4 179.5 all-gather.2
  193.1 139.8 all-gather.4
  449.4 154.9 reduce-scatter.1
